TPU v7x, 128 devices: a whole 4x4x4 slice. The times are simulated.
128 devices in a mesh: dp: 8 (over x, y_lo), expert: 16 (over z, y_hi, core).
Axes of the slice: x: 4, y: 4 (y_hi: 2, y_lo: 2; y = y_hi * 2 + y_lo), z: 4, core: 2. Of those that a mesh axis runs over, the one named last changes fastest.
Arguments:
- tokens: bfloat16 [16384, 3072], P(('dp', 'expert')), parts along dimension 0, may hold values from -6 to 6
- expert_ids: int32 [16384, 4], P(('dp', 'expert')), parts along dimension 0, may hold values from 0 to 15, as said below
- gate_weights: float32 [16384, 4], P(('dp', 'expert')), parts along dimension 0, may hold values from 0.05 to 0.5
- slot_rows: int32 [128, 16, 64], P(('dp', 'expert')), parts along dimension 0, may hold values from 0 to 128, as said below
- w_in: bfloat16 [16, 3072, 2560], P('expert'), may hold values from -0.109375 to 0.109375
- w_out: bfloat16 [16, 1280, 3072], P('expert'), may hold values from -0.15625 to 0.15625
Outputs:
- mixed: bfloat16 [16384, 3072], P(('dp', 'expert')), parts along dimension 0
There are 8 independent parts, one for each index of `dp`. A program takes and returns all parts, laid end to end along the dimension named above; an argument that names none is the same for every part. Nothing has to cross between parts.
Inputs may be any that keep to these rules, and one draw needn't show every extreme that they name: `expert_ids`: each row names 4 different experts. slot_rows[s, e] lists, in increasing order, the rows of shard s whose tokens name expert e, the first 64 of them, then 128 in the remaining slots; in every draw some expert has all 64 slots filled by every shard.
All inputs are finite; a program needn't handle non-finite values.
Results may differ from a plain program's by a relative error of at most 0.0063.
Values may be sent and summed in bfloat16 or wider, within the bound.
No kernel may reach another device: no remote copies, remote signals or barrier semaphores. Data moves between devices by JAX's collectives and lax.ppermute only.
A program may use at most 128 MiB of HBM per device.

v0:
```python
import jax
import jax.numpy as jnp
from jax import lax
from jax.sharding import PartitionSpec as P


def expert_block(rows_in, w_first, w_second):
    features = rows_in.shape[-1]
    hidden_units = w_second.shape[0]
    flat = rows_in.reshape(-1, features)
    projected = jnp.dot(flat, w_first, preferred_element_type=jnp.float32)
    intermediate_activation = (
        jax.nn.silu(projected[:, :hidden_units]) * projected[:, hidden_units:]
    ).astype(jnp.bfloat16)
    result = jnp.dot(intermediate_activation, w_second, preferred_element_type=jnp.float32).astype(
        jnp.bfloat16
    )
    return result.reshape(rows_in.shape)


def shards(tokens, expert_ids, gate_weights, slot_rows, w_in, w_out):
    tok_rows, features = tokens.shape
    experts = slot_rows.shape[1]
    capacity = slot_rows.shape[2]
    w_first = w_in[0]
    w_second = w_out[0]
    own_rows = slot_rows[0]
    occupied = own_rows < tok_rows
    clipped = jnp.minimum(own_rows, tok_rows - 1)
    matches = (
        expert_ids[:, :, None] == jnp.arange(experts, dtype=jnp.int32)[None, None, :]
    ).astype(jnp.float32)
    gate_of = jnp.einsum("tk,tke->et", gate_weights, matches)
    slot_gate = jnp.where(occupied, jnp.take_along_axis(gate_of, clipped, axis=1), 0.0).astype(
        jnp.bfloat16
    )
    this_device = lax.axis_index("expert")
    gathered, all_lists = (
        lax.all_gather(tokens, "expert", axis=0, tiled=True),
        lax.all_gather(slot_rows, "expert", axis=0, tiled=True),
    )
    own_lists = lax.dynamic_index_in_dim(all_lists, this_device, axis=1, keepdims=False)
    offsets = jnp.arange(experts, dtype=jnp.int32)[:, None] * tok_rows
    positions = jnp.where(own_lists < tok_rows, own_lists + offsets, gathered.shape[0])
    selected = jnp.take(gathered, positions.reshape(-1), axis=0, mode="fill", fill_value=0)
    layer_response = expert_block(selected.reshape(experts, capacity, features), w_first, w_second)
    returned = lax.all_to_all(layer_response, "expert", split_axis=0, concat_axis=0, tiled=True)
    expert_onehot = own_rows.reshape(-1)[None, :] == jnp.arange(tok_rows, dtype=jnp.int32)[:, None]
    mixing = jnp.where(expert_onehot, slot_gate.reshape(-1)[None, :], jnp.zeros((), jnp.bfloat16))
    summed = jnp.dot(mixing, returned.reshape(-1, features), preferred_element_type=jnp.float32)
    return summed.astype(jnp.bfloat16)


def solution(mesh):
    in_specs = (
        P(("dp", "expert"), None),
        P(("dp", "expert"), None),
        P(("dp", "expert"), None),
        P(("dp", "expert"), None, None),
        P("expert", None, None),
        P("expert", None, None),
    )
    out_specs = P(("dp", "expert"), None)
    return jax.shard_map(shards, mesh=mesh, in_specs=in_specs, out_specs=out_specs, check_vma=False)
```

profile of v0, /device:TPU:1, one launch (start us, length us, event | category | flops | bytes accessed | tf_op | source)
XLA Modules:
  0.0 244.3 jit_solution(8252859320478719966)
XLA Ops:
  6.5 0.7 all-gather.2.cloned.1.call-update
  7.3 0.1 add.75
  7.3 0.1 add.79
  7.4 0.1 add.76
  7.5 28.1 %all_gather.6 = s32[16,16,64]{2,1,0:T(8,128)S(1)} all-gather(s32[1,16,64]{2,1,0:T(8,128)} %param.9), channel_id=1, replica_groups=mesh['dp'=8,'expert'=16] {'expert'}, dimensions={0}, use_global_device_ids=true | all-gather | bytes 69632 | tf_op jit(solution)/shard_map/all_gather | solution.py:40
  35.6 0.5 broadcast.165
  36.1 0.7 fusion.26
  36.8 0.1 squeeze.13
  36.9 0.1 squeeze.14
  37.0 67.5 %all-gather.2.cloned.1.call-done = bf16[2048,3072]{1,0:T(8,128)(2,1)} async-done(((bf16[128,3072]{1,0:T(8,128)(2,1)}), bf16[2048,3072]{1,0:T(8,128)(2,1)}) %all-gather.2.cloned.1.call-update) | async-done | bytes 12582928 | tf_op jit(solution)/shard_map/all_gather | solution.py:39
  104.5 18.4 %gather_fusion = bf16[1024,3072]{1,0:T(8,128)(2,1)} fusion(bf16[2048,3072]{1,0:T(8,128)(2,1)} %all-gather.2.cloned.1.call-done, s32[1024]{0:T(1024)S(1)} %broadcast_clamp_fusion), kind=kCustom, calls=%fused_computation | custom fusion | bytes 12587008 | tf_op jit(solution)/shard_map/jit(_take)/gather | solution.py:45
  122.9 21.2 %fusion = f32[1024,2560]{1,0:T(8,128)S(1)} fusion(bf16[1,3072,2560]{2,1,0:T(8,128)(2,1)} %param.10, bf16[1024,3072]{1,0:T(8,128)(2,1)} %gather_fusion, pred[1024]{0:T(1024)(128)(4,1)S(1)} %compare_and_fusion), kind=kOutput, calls=%fused_computation.2 | convolution fusion | flops 16109273088 | bytes 32506880 | tf_op jit(solution)/shard_map/dot_general | solution.py:11
  144.1 0.0 copy-done.3
  144.1 10.3 %fusion.6 = bf16[1024,3072]{1,0:T(8,128)(2,1)} fusion(bf16[1,1280,3072]{2,1,0:T(8,128)(2,1)S(1)} %copy-done.3, f32[1024,2560]{1,0:T(8,128)S(1)} %fusion), kind=kOutput, calls=%fused_computation.8 | convolution fusion | flops 8064073728 | bytes 24641536 | tf_op jit(solution)/shard_map/dot_general | solution.py:15
  154.4 4.7 %all-to-all-start = ((bf16[16,64,3072]{2,1,0:T(8,128)(2,1)}), bf16[16,64,3072]{2,1,0:T(8,128)(2,1)}, u32[]{:S(2)}, u32[]{:S(2)}) async-start(bf16[16,64,3072]{2,1,0:T(8,128)(2,1)} %bitcast.24), calls=%async_computation | async-start | bytes 12582912 | tf_op jit(solution)/shard_map/all_to_all | solution.py:47
  159.1 0.1 eq.28
  159.2 0.1 reshape.124
  159.3 0.0 copy-done.1
  159.3 0.1 copy.9
  159.4 0.2 copy.10
  159.6 0.4 fusion.16
  159.9 7.3 %gather_fusion.1 = bf16[1024]{0:T(1024)(128)(2,1)S(1)} fusion(f32[16,128]{0,1:T(8,128)S(1)} %bitcast.23, s32[1024]{0:T(1024)S(1)} %reshape.124), kind=kCustom, calls=%fused_computation.1 | custom fusion | bytes 12288 | tf_op jit(solution)/shard_map/jit(take_along_axis)/gather | solution.py:34
  167.2 65.6 %all-to-all-done = bf16[16,64,3072]{2,1,0:T(8,128)(2,1)} async-done(((bf16[16,64,3072]{2,1,0:T(8,128)(2,1)}), bf16[16,64,3072]{2,1,0:T(8,128)(2,1)}, u32[]{:S(2)}, u32[]{:S(2)}) %all-to-all-start) | async-done | bytes 6291488 | tf_op jit(solution)/shard_map/all_to_all | solution.py:47
  232.8 4.7 %convolution_convert_fusion = bf16[128,3072]{1,0:T(8,128)(2,1)} fusion(bf16[1024,3072]{1,0:T(8,128)(2,1)} %bitcast.9, s32[1024]{0:T(1024)S(1)} %eq.28, bf16[1024]{0:T(1024)(128)(2,1)S(1)} %select_convert_fusion), kind=kOutput, calls=%fused_computation.11 | convolution fusion | flops 805961728 | bytes 7084032 | tf_op jit(solution)/shard_map/dot_general | solution.py:50
  (13 shorter events, 0.1 us)
Async XLA Ops:
  6.5 98.0 %all-gather.2.cloned.1.call-start = ((), (), s32[]{:S(2)}) async-start(), calls=%async_computation.1 | async-start | bytes 13369344 | tf_op jit(solution)/shard_map/all_gather | solution.py:39
  122.9 21.2 %copy-start.3 = (bf16[1,1280,3072]{2,1,0:T(8,128)(2,1)S(1)}, bf16[1,1280,3072]{2,1,0:T(8,128)(2,1)}, u32[]{:S(2)}) copy-start(bf16[1,1280,3072]{2,1,0:T(8,128)(2,1)} %param.11) | copy-start | bytes 23592964
  154.4 4.7 %copy-start = (s32[1,16,64]{2,1,0:T(8,128)S(1)}, s32[1,16,64]{2,1,0:T(8,128)}, u32[]{:S(2)}) copy-start(s32[1,16,64]{2,1,0:T(8,128)} %param.9) | copy-start | bytes 12292
  154.4 4.9 %copy-start.1 = (s32[128,4]{0,1:T(4,128)S(1)}, s32[128,4]{0,1:T(4,128)}, u32[]{:S(2)}) copy-start(s32[128,4]{0,1:T(4,128)} %param.7) | copy-start | bytes 6148
  154.4 5.0 %copy-start.2 = (f32[128,4]{0,1:T(4,128)S(1)}, f32[128,4]{0,1:T(4,128)}, u32[]{:S(2)}) copy-start(f32[128,4]{0,1:T(4,128)} %param.8) | copy-start | bytes 6148
  154.4 78.4 %all-to-all-start = ((bf16[16,64,3072]{2,1,0:T(8,128)(2,1)}), bf16[16,64,3072]{2,1,0:T(8,128)(2,1)}, u32[]{:S(2)}, u32[]{:S(2)}) async-start(bf16[16,64,3072]{2,1,0:T(8,128)(2,1)} %bitcast.24), calls=%async_computation | async-start | bytes 12582912 | tf_op jit(solution)/shard_map/all_to_all | solution.py:47
Sparse Core Ops, SparseCore 0:
  9.8 94.6 all-gather.1
where the time goes:
time: 245 us; the launch traced here: 244 us
  waiting for transfers between devices  134 us (55%)
  matrix products  36.5 us (15%)
  blocking collectives  28.1 us (11%)
  local copies, waits for them, and re-layouts  27.6 us (11%)
  between operations  13.5 us (6%)
  starting transfers between devices  4.74 us (2%)
    all_gather x1, waiting for transfers between devices, shards(): lax.all_gather(tokens, 'expert', axis=0, tiled=True)  67.5 us
    all_to_all x1, waiting for transfers between devices, shards(): lax.all_to_all(layer_response, 'expert', split_axis=0, concat_axis=0, til...  65.6 us
    all_gather x1, blocking collectives, shards(): lax.all_gather(slot_rows, 'expert', axis=0, tiled=True)  28.1 us
    dot_general x1, matrix products, expert_block(): projected = jnp.dot(flat, w_first, preferred_element_type=jnp.float32)  21.2 us
    gather x1, local copies, waits for them, and re-layouts, shards(): jnp.take(gathered, positions.reshape(-1), axis=0, mode='fill', fill_value=0)  18.4 us
    dot_general x1, matrix products, expert_block(): jnp.dot(intermediate_activation, w_second, preferred_element_type=jnp.flo...  10.3 us
    gather x2, local copies, waits for them, and re-layouts, shards(): jnp.take_along_axis(gate_of, clipped, axis=1)  7.32 us
  transfers between devices with their start and end apart: 2, of which 2 were waited for; matrix products, arithmetic and copies ran while one was open for 4% of the time, Pallas kernels for 0%

commit v1 on v0

--- a/solution.py
+++ b/solution.py
@@ -36,7 +36,9 @@
     )
     this_device = lax.axis_index("expert")
     gathered, all_lists = (
-        lax.all_gather(tokens, "expert", axis=0, tiled=True),
+        jnp.concatenate(
+            lax.all_to_all(jnp.stack([tokens] * lax.axis_size("expert")), "expert", 0, 0), axis=0
+        ),
         lax.all_gather(slot_rows, "expert", axis=0, tiled=True),
     )
     own_lists = lax.dynamic_index_in_dim(all_lists, this_device, axis=1, keepdims=False)

time: 245 us -> 310 us (1.27)
  blocking collectives: 28.1 us -> 155 us
  waiting for transfers between devices: 134 us -> 65.6 us
  between operations: 13.5 us -> 0.1 us
  starting transfers between devices: 4.74 us -> 14.3 us
  local copies, waits for them, and re-layouts: 27.6 us -> 34.8 us
  matrix products: 36.5 us -> 39.8 us
    all_gather x1, blocking collectives: 28.1 us -> 155 us  [shards(): lax.all_gather(slot_rows, 'expert', axis=0, tiled=True)]
    all_gather x1 -> x0, waiting for transfers between devices: 67.5 us -> none  [shards(): lax.all_gather(tokens, 'expert', axis=0, tiled=True)]
    all_to_all x0 -> x1, starting transfers between devices: none -> 9.59 us  [shards(): lax.all_to_all(jnp.stack([tokens] * lax.axis_size('expert')), 'expert', 0...]
    another operation x0 -> x1, local copies, waits for them, and re-layouts: none -> 7.21 us  [shards(): jnp.stack([tokens] * lax.axis_size('expert'))]
    dot_general x1, matrix products: 10.3 us -> 13.7 us  [expert_block(): jnp.dot(intermediate_activation, w_second, preferred_element_type=jnp.flo...]
  transfers between devices with their start and end apart: 2 -> 2, of which waited for: 2 -> 1; matrix products, arithmetic and copies ran while one was open for 4% -> 3% of each run, Pallas kernels for 0% -> 0%
where the time goes in v1:
time: 310 us; the launch traced here: 309 us
  blocking collectives  155 us (50%)
  waiting for transfers between devices  65.6 us (21%)
  matrix products  39.8 us (13%)
  local copies, waits for them, and re-layouts  34.8 us (11%)
  starting transfers between devices  14.3 us (5%)
    all_gather x1, blocking collectives, shards(): lax.all_gather(slot_rows, 'expert', axis=0, tiled=True)  155 us
    all_to_all x1, waiting for transfers between devices, shards(): lax.all_to_all(layer_response, 'expert', split_axis=0, concat_axis=0, til...  65.6 us
    dot_general x1, matrix products, expert_block(): projected = jnp.dot(flat, w_first, preferred_element_type=jnp.float32)  21.1 us
    gather x1, local copies, waits for them, and re-layouts, shards(): jnp.take(gathered, positions.reshape(-1), axis=0, mode='fill', fill_value=0)  18.4 us
    dot_general x1, matrix products, expert_block(): jnp.dot(intermediate_activation, w_second, preferred_element_type=jnp.flo...  13.7 us
    all_to_all x1, starting transfers between devices, shards(): lax.all_to_all(jnp.stack([tokens] * lax.axis_size('expert')), 'expert', 0...  9.59 us
    gather x2, local copies, waits for them, and re-layouts, shards(): jnp.take_along_axis(gate_of, clipped, axis=1)  7.32 us
    another operation x1, local copies, waits for them, and re-layouts, shards(): jnp.stack([tokens] * lax.axis_size('expert'))  7.21 us
  transfers between devices with their start and end apart: 2, of which 1 were waited for; matrix products, arithmetic and copies ran while one was open for 3% of the time, Pallas kernels for 0%

profile of v1, /device:TPU:1, one launch (start us, length us, event | category | flops | bytes accessed | tf_op | source)
XLA Modules:
  0.0 309.4 jit_solution(4084966006928889066)
XLA Ops:
  0.0 7.2 %stack.2 = bf16[16,128,3072]{2,1,0:T(8,128)(2,1)} broadcast(bf16[128,3072]{1,0:T(8,128)(2,1)} %param.6), dimensions={1,2} | broadcast | bytes 13369344 | tf_op jit(solution)/shard_map/stack | solution.py:40
  7.2 9.6 %all-to-all-start = ((bf16[16,128,3072]{2,1,0:T(8,128)(2,1)}), bf16[16,128,3072]{2,1,0:T(8,128)(2,1)}, u32[]{:S(2)}, u32[]{:S(2)}) async-start(bf16[16,128,3072]{2,1,0:T(8,128)(2,1)} %stack.2), calls=%async_computation | async-start | bytes 25165824 | tf_op jit(solution)/shard_map/all_to_all | solution.py:40
  16.8 0.1 add.75
  16.9 0.1 add.79
  17.0 0.1 add.76
  17.0 0.0 copy-done
  17.0 154.8 %all_gather.3 = s32[16,16,64]{2,1,0:T(8,128)S(1)} all-gather(s32[1,16,64]{2,1,0:T(8,128)S(1)} %copy-done), channel_id=1, replica_groups=mesh['dp'=8,'expert'=16] {'expert'}, dimensions={0}, use_global_device_ids=true | all-gather | bytes 69632 | tf_op jit(solution)/shard_map/all_gather | solution.py:42
  171.9 0.5 broadcast.167
  172.4 0.7 fusion.26
  173.1 0.1 squeeze.14
  173.1 0.1 squeeze.13
  173.3 0.0 all-to-all-done
  173.3 18.4 %gather_fusion = bf16[1024,3072]{1,0:T(8,128)(2,1)} fusion(bf16[2048,3072]{1,0:T(8,128)(2,1)} %bitcast.5, s32[1024]{0:T(1024)S(1)} %broadcast_clamp_fusion), kind=kCustom, calls=%fused_computation | custom fusion | bytes 12587008 | tf_op jit(solution)/shard_map/jit(_take)/gather | solution.py:47
  191.7 21.1 %fusion = f32[1024,2560]{1,0:T(8,128)S(1)} fusion(bf16[1,3072,2560]{2,1,0:T(8,128)(2,1)} %param.10, bf16[1024,3072]{1,0:T(8,128)(2,1)} %gather_fusion, pred[1024]{0:T(1024)(128)(4,1)S(1)} %compare_and_fusion), kind=kOutput, calls=%fused_computation.2 | convolution fusion | flops 16109273088 | bytes 32506880 | tf_op jit(solution)/shard_map/dot_general | solution.py:11
  212.7 13.7 %fusion.6 = bf16[1024,3072]{1,0:T(8,128)(2,1)} fusion(bf16[1,1280,3072]{2,1,0:T(8,128)(2,1)} %param.11, f32[1024,2560]{1,0:T(8,128)S(1)} %fusion), kind=kOutput, calls=%fused_computation.8 | convolution fusion | flops 8064073728 | bytes 24641536 | tf_op jit(solution)/shard_map/dot_general | solution.py:15
  226.5 4.7 %all-to-all-start.1 = ((bf16[16,64,3072]{2,1,0:T(8,128)(2,1)}), bf16[16,64,3072]{2,1,0:T(8,128)(2,1)}, u32[]{:S(2)}, u32[]{:S(2)}) async-start(bf16[16,64,3072]{2,1,0:T(8,128)(2,1)} %bitcast.25), calls=%async_computation.1 | async-start | bytes 12582912 | tf_op jit(solution)/shard_map/all_to_all | solution.py:49
  231.1 0.1 eq.28
  231.2 0.2 copy.10
  231.4 0.1 copy.9
  231.5 0.1 reshape.130
  231.6 0.3 fusion.16
  231.9 7.3 %gather_fusion.1 = bf16[1024]{0:T(1024)(128)(2,1)S(1)} fusion(f32[16,128]{0,1:T(8,128)S(1)} %bitcast.24, s32[1024]{0:T(1024)S(1)} %reshape.130), kind=kCustom, calls=%fused_computation.1 | custom fusion | bytes 12288 | tf_op jit(solution)/shard_map/jit(take_along_axis)/gather | solution.py:34
  239.2 65.6 %all-to-all-done.1 = bf16[16,64,3072]{2,1,0:T(8,128)(2,1)} async-done(((bf16[16,64,3072]{2,1,0:T(8,128)(2,1)}), bf16[16,64,3072]{2,1,0:T(8,128)(2,1)}, u32[]{:S(2)}, u32[]{:S(2)}) %all-to-all-start.1) | async-done | bytes 6291488 | tf_op jit(solution)/shard_map/all_to_all | solution.py:49
  304.8 4.7 %convolution_convert_fusion = bf16[128,3072]{1,0:T(8,128)(2,1)} fusion(bf16[1024,3072]{1,0:T(8,128)(2,1)} %bitcast.10, s32[1024]{0:T(1024)S(1)} %eq.28, bf16[1024]{0:T(1024)(128)(2,1)S(1)} %select_convert_fusion), kind=kOutput, calls=%fused_computation.11 | convolution fusion | flops 805961728 | bytes 7084032 | tf_op jit(solution)/shard_map/dot_general | solution.py:52
  (11 shorter events, 0.1 us)
Async XLA Ops:
  7.2 9.8 %copy-start = (s32[1,16,64]{2,1,0:T(8,128)S(1)}, s32[1,16,64]{2,1,0:T(8,128)}, u32[]{:S(2)}) copy-start(s32[1,16,64]{2,1,0:T(8,128)} %param.9) | copy-start | bytes 12292
  7.2 166.1 %all-to-all-start = ((bf16[16,128,3072]{2,1,0:T(8,128)(2,1)}), bf16[16,128,3072]{2,1,0:T(8,128)(2,1)}, u32[]{:S(2)}, u32[]{:S(2)}) async-start(bf16[16,128,3072]{2,1,0:T(8,128)(2,1)} %stack.2), calls=%async_computation | async-start | bytes 25165824 | tf_op jit(solution)/shard_map/all_to_all | solution.py:40
  226.5 4.8 %copy-start.1 = (f32[128,4]{0,1:T(4,128)S(1)}, f32[128,4]{0,1:T(4,128)}, u32[]{:S(2)}) copy-start(f32[128,4]{0,1:T(4,128)} %param.8) | copy-start | bytes 6148
  226.5 4.9 %copy-start.2 = (s32[128,4]{0,1:T(4,128)S(1)}, s32[128,4]{0,1:T(4,128)}, u32[]{:S(2)}) copy-start(s32[128,4]{0,1:T(4,128)} %param.7) | copy-start | bytes 6148
  226.5 78.3 %all-to-all-start.1 = ((bf16[16,64,3072]{2,1,0:T(8,128)(2,1)}), bf16[16,64,3072]{2,1,0:T(8,128)(2,1)}, u32[]{:S(2)}, u32[]{:S(2)}) async-start(bf16[16,64,3072]{2,1,0:T(8,128)(2,1)} %bitcast.25), calls=%async_computation.1 | async-start | bytes 12582912 | tf_op jit(solution)/shard_map/all_to_all | solution.py:49
